TPU v7x, 32 devices: a whole 2x2x4 slice. The times are simulated.
32 devices in a mesh: groups: 2 (over x), seq: 16 (over z, y, core).
Axes of the slice: x: 2, y: 2, z: 4, core: 2. Of those that a mesh axis runs over, the one named last changes fastest.
Arguments:
- clean: bfloat16 [8192, 2048], P(('groups', 'seq')), parts along dimension 0, may hold values from -6 to 6
- delta: bfloat16 [8192, 2048], P(('groups', 'seq')), parts along dimension 0, may hold values from -0.25 to 0.25
- cotangent: bfloat16 [8192, 1024], P(('groups', 'seq')), parts along dimension 0, may hold values from -6 to 6
- w_query: bfloat16 [2048, 1024], P('seq'), may hold values from -0.125 to 0.125
- w_key: bfloat16 [2048, 1024], P('seq'), may hold values from -0.125 to 0.125
- w_value: bfloat16 [2048, 1024], P('seq'), may hold values from -0.125 to 0.125
- masks: int32 [32, 2, 2], P(('groups', 'seq')), parts along dimension 0, may hold values 0 or 1
Outputs:
- output: bfloat16 [8192, 1024], P(('groups', 'seq')), parts along dimension 0
- grad_input: bfloat16 [8192, 2048], P(('groups', 'seq')), parts along dimension 0
There are 2 independent parts, one for each index of `groups`. A program takes and returns all parts, laid end to end along the dimension named above; an argument that names none is the same for every part. Nothing has to cross between parts.
All inputs are finite; a program needn't handle non-finite values. No bound on the sum of `masks` on one device may be relied on, other than what follows from the above.
Results may differ from a plain program's by a relative error of at most 0.012.
Values may be sent and summed in bfloat16 or wider, within the bound.
No kernel may reach another device: no remote copies, remote signals or barrier semaphores. Data moves between devices by JAX's collectives and lax.ppermute only.
A program may use at most 128 MiB of HBM per device.

v0:
```python
import jax
import jax.numpy as jnp
from jax import lax
from jax.sharding import PartitionSpec as P

NH = 8
DH = 128
BLK = 128
EPSILON = 1e-06


def carried_in(shard, axis, combine, identity, reverse):
    peers, index = (lax.axis_size(axis), lax.axis_index(axis))
    everything = lax.all_gather(shard, axis)
    start = jnp.broadcast_to(jnp.asarray(identity, shard.dtype), shard.shape)

    def turn(k, before):
        at = peers - 1 - k if reverse else k
        reached = at > index if reverse else at < index
        new = combine(before, everything[at])
        return jnp.where(reached, new, before)

    return lax.fori_loop(0, peers, turn, start)


def allowed_pairs(blocks, width):
    count = blocks.shape[0]
    row = jnp.arange(count)[:, None]
    col = jnp.arange(count)[None, :]
    inner_row = jnp.arange(width)[:, None]
    inner_col = jnp.arange(width)[None, :]
    lower = (row > col).astype(jnp.float32)[:, :, None, None]
    same = (row == col).astype(jnp.float32)[:, :, None, None] * (inner_row >= inner_col).astype(
        jnp.float32
    )[None, None]
    return blocks.astype(jnp.float32)[:, :, None, None] * (lower + same)


def add_states(earlier, later_one):
    return earlier + later_one


def on_device(clean, delta, cotangent, w_query, w_key, w_value, masks):
    tok_rows = clean.shape[0]
    features = w_query.shape[1]
    blocks_here = tok_rows // BLK
    f32 = jnp.float32
    x_in = (clean.astype(f32) + delta.astype(f32)).astype(jnp.bfloat16)
    w_cat = jnp.concatenate([w_query, w_key, w_value], axis=1)
    full_weights = lax.all_gather(w_cat, "seq", axis=0, tiled=True)
    projected = jnp.dot(x_in, full_weights, preferred_element_type=f32)
    projected = projected.astype(jnp.bfloat16)
    query = projected[:, :features].reshape(blocks_here, BLK, NH, DH)
    key = projected[:, features : 2 * features].reshape(blocks_here, BLK, NH, DH)
    value = projected[:, 2 * features :].reshape(blocks_here, BLK, NH, DH)
    zero_state = jnp.zeros((NH, DH, DH), f32)
    state_local = jnp.einsum("ibhd,ibhe->hde", key, value, preferred_element_type=f32)
    state = carried_in(state_local, "seq", add_states, zero_state, False)
    state_b = state.astype(jnp.bfloat16)
    allow = allowed_pairs(masks[0], BLK)
    scores = jnp.einsum("ibhd,jchd->hijbc", query, key, preferred_element_type=f32)
    attn = (scores * allow).astype(jnp.bfloat16)
    mixed = jnp.einsum("hijbc,jchd->ibhd", attn, value, preferred_element_type=f32)
    mixed = mixed + jnp.einsum("ibhd,hde->ibhe", query, state_b, preferred_element_type=f32)
    root = jnp.sqrt(jnp.mean(mixed * mixed, axis=-1, keepdims=True) + EPSILON)
    normed = mixed / root
    output = normed.astype(jnp.bfloat16).reshape(tok_rows, features)
    grad_out = cotangent.astype(f32).reshape(blocks_here, BLK, NH, DH)
    d_mixed = (grad_out - normed * jnp.mean(grad_out * normed, axis=-1, keepdims=True)) / root
    d_mixed_b = d_mixed.astype(jnp.bfloat16)
    grad_local = jnp.einsum("ibhd,ibhe->hde", query, d_mixed_b, preferred_element_type=f32)
    later = carried_in(grad_local, "seq", add_states, zero_state, True)
    later_b = later.astype(jnp.bfloat16)
    d_attn = (
        jnp.einsum("ibhe,jche->hijbc", d_mixed_b, value, preferred_element_type=f32) * allow
    ).astype(jnp.bfloat16)
    d_query = jnp.einsum("hijbc,jchd->ibhd", d_attn, key, preferred_element_type=f32)
    d_query = d_query + jnp.einsum("ibhe,hde->ibhd", d_mixed_b, state_b, preferred_element_type=f32)
    d_key = jnp.einsum("hijbc,ibhd->jchd", d_attn, query, preferred_element_type=f32)
    d_key = d_key + jnp.einsum("jche,hde->jchd", value, later_b, preferred_element_type=f32)
    d_value = jnp.einsum("hijbc,ibhe->jche", attn, d_mixed_b, preferred_element_type=f32)
    d_value = d_value + jnp.einsum("jchd,hde->jche", key, later_b, preferred_element_type=f32)
    d_proj = jnp.concatenate(
        [
            d_query.reshape(tok_rows, features),
            d_key.reshape(tok_rows, features),
            d_value.reshape(tok_rows, features),
        ],
        axis=1,
    ).astype(jnp.bfloat16)
    grad_input = lax.dot_general(
        d_proj, full_weights, (((1,), (1,)), ((), ())), preferred_element_type=f32
    )
    return (output, grad_input.astype(jnp.bfloat16))


def solution(mesh):
    return jax.shard_map(
        on_device,
        mesh=mesh,
        in_specs=(
            P(("groups", "seq"), None),
            P(("groups", "seq"), None),
            P(("groups", "seq"), None),
            P("seq", None),
            P("seq", None),
            P("seq", None),
            P(("groups", "seq"), None, None),
        ),
        out_specs=(P(("groups", "seq"), None), P(("groups", "seq"), None)),
        check_vma=False,
    )
```

profile of v0, /device:TPU:0, one launch (start us, length us, event | category | flops | bytes accessed | tf_op | source)
XLA Modules:
  0.0 334.4 jit_solution(9458282480844987957)
XLA Ops:
  7.2 2.2 pad_maximum_fusion
  9.5 104.9 %all-gather.6.cloned.1.call-done = bf16[2048,3072]{1,0:T(8,128)(2,1)} async-done(((bf16[128,3072]{1,0:T(8,128)(2,1)}), bf16[2048,3072]{1,0:T(8,128)(2,1)}) %all-gather.6.cloned.1.call-update) | async-done | bytes 12582928 | tf_op jit(solution)/shard_map/all_gather | solution.py:50
  114.4 8.0 %convolution_convert_fusion = bf16[256,3072]{1,0:T(8,128)(2,1)S(1)} fusion(bf16[2048,3072]{1,0:T(8,128)(2,1)} %all-gather.6.cloned.1.call-done, bf16[256,2048]{1,0:T(8,128)(2,1)S(1)} %copy-done.12, bf16[256,2048]{1,0:T(8,128)(2,1)S(1)} %copy-done.13), kind=kOutput, calls=%fused_computation.2 | convolution fusion | flops 3224109056 | bytes 16252928 | tf_op jit(solution)/shard_map/dot_general | solution.py:51
  122.7 1.1 convolution_bitcast_fusion.5
  124.2 1.1 convert_bitcast_fusion
  125.4 1.2 copy.135
  126.6 1.6 copy.70
  130.0 1.4 copy.101
  131.4 0.9 bitcast_bitcast_fusion.1
  132.3 2.1 copy.96
  134.4 2.1 copy.79
  136.6 1.7 fusion.1
  138.3 1.0 copy-done
  139.3 1.3 convolution_bitcast_fusion
  140.6 56.5 %all-gather.8.cloned.1.call-done = f32[128,128,128]{2,1,0:T(8,128)} async-done(((f32[8,128,128]{2,1,0:T(8,128)}), f32[128,128,128]{2,1,0:T(8,128)}) %all-gather.8.cloned.1.call-update) | async-done | bytes 8388624 | tf_op jit(solution)/shard_map/all_gather | solution.py:14
  197.1 20.1 %while.30 = (s32[]{:T(128)}, f32[8,128,128]{2,1,0:T(8,128)S(1)}, s32[]{:T(128)}, f32[16,8,128,128]{3,2,1,0:T(8,128)}, s32[]{:T(128)}, /*index=5*/s32[]{:T(128)}) while((s32[]{:T(128)}, f32[8,128,128]{2,1,0:T(8,128)S(1)}, s32[]{:T(128)}, f32[16,8,128,128]{3,2,1,0:T(8,128)}, s32[]{:T(128)}, /*index=5*/s32[]{:T(128)}) %tuple.88), condition=%wide.region_1.2_spmd.clone, body=%wide.region_0.1_spmd.clone.sunk | while | flops 393220 | bytes 1572957 | solution.py:23
  197.1 1.3 add_select_fusion.4
  198.4 1.2 add_select_fusion.4
  199.7 1.2 add_select_fusion.4
  200.9 1.2 add_select_fusion.4
  202.2 1.2 add_select_fusion.4
  203.4 1.2 add_select_fusion.4
  204.7 1.2 add_select_fusion.4
  205.9 1.2 add_select_fusion.4
  207.2 1.2 add_select_fusion.4
  208.4 1.2 add_select_fusion.4
  209.7 1.2 add_select_fusion.4
  210.9 1.2 add_select_fusion.4
  212.2 1.2 add_select_fusion.4
  213.4 1.2 add_select_fusion.4
  214.7 1.2 add_select_fusion.4
  215.9 1.2 add_select_fusion.4
  217.2 1.6 multiply_reduce_fusion.1
  219.0 1.1 divide_convert_fusion
  220.1 1.1 convolution_bitcast_fusion.4
  221.3 1.5 fusion
  222.7 1.4 convolution_bitcast_fusion.3
  224.1 1.1 fusion.13
  225.2 2.2 copy.76
  227.3 2.0 copy.159
  229.3 2.1 copy.68
  231.4 2.0 copy.160
  233.4 1.4 convolution_bitcast_fusion.2
  235.4 59.2 %all-gather.10.cloned.1.call-done = f32[128,128,128]{2,1,0:T(8,128)} async-done(((f32[8,128,128]{2,1,0:T(8,128)}), f32[128,128,128]{2,1,0:T(8,128)}) %all-gather.10.cloned.1.call-update) | async-done | bytes 8388624 | tf_op jit(solution)/shard_map/all_gather | solution.py:14
  294.5 20.2 %while.31 = (s32[]{:T(128)}, f32[8,128,128]{2,1,0:T(8,128)S(1)}, s32[]{:T(128)}, f32[16,8,128,128]{3,2,1,0:T(8,128)}, s32[]{:T(128)}, /*index=5*/s32[]{:T(128)}, s32[]{:T(128)}, s32[]{:T(128)}) while((s32[]{:T(128)}, f32[8,128,128]{2,1,0:T(8,128)S(1)}, s32[]{:T(128)}, f32[16,8,128,128]{3,2,1,0:T(8,128)}, s32[]{:T(128)}, ...), condition=%wide.region_5.6_spmd.clone, body=%wide.region_4.5_spmd.clone.sunk | while | flops 393224 | bytes 1573019 | solution.py:23
  294.5 1.3 add_select_fusion.5
  295.9 1.2 add_select_fusion.5
  297.1 1.2 add_select_fusion.5
  298.4 1.2 add_select_fusion.5
  299.6 1.2 add_select_fusion.5
  300.9 1.2 add_select_fusion.5
  302.2 1.2 add_select_fusion.5
  303.4 1.2 add_select_fusion.5
  304.7 1.2 add_select_fusion.5
  305.9 1.2 add_select_fusion.5
  307.2 1.2 add_select_fusion.5
  308.4 1.2 add_select_fusion.5
  309.7 1.2 add_select_fusion.5
  311.0 1.2 add_select_fusion.5
  312.2 1.2 add_select_fusion.5
  313.5 1.2 add_select_fusion.5
  314.7 1.5 fusion.12
  316.6 0.9 copy.158
  318.9 9.0 %convolution_convert_fusion.1 = bf16[256,2048]{1,0:T(8,128)(2,1)} fusion(bf16[2048,3072]{1,0:T(8,128)(2,1)} %all-gather.6.cloned.1.call-done, bf16[256,1024]{1,0:T(8,128)(2,1)S(1)} %bitcast.167, bf16[256,1024]{1,0:T(8,128)(2,1)S(1)} %bitcast.166, bf16[256,1024]{1,0:T(8,128)(2,1)S(1)} %bitcast.165), kind=kOutput, calls=%fused_computation.3 | convolution fusion | flops 3226468352 | bytes 15204352 | tf_op jit(solution)/shard_map/dot_general | solution.py:91
  (54 shorter events, 5.1 us)
Async XLA Ops:
  7.2 107.2 %copy-start.13 = (bf16[256,2048]{1,0:T(8,128)(2,1)S(1)}, bf16[256,2048]{1,0:T(8,128)(2,1)}, u32[]{:S(2)}) copy-start(bf16[256,2048]{1,0:T(8,128)(2,1)} %param.11) | copy-start | bytes 3145732
  7.2 107.2 %copy-start.12 = (bf16[256,2048]{1,0:T(8,128)(2,1)S(1)}, bf16[256,2048]{1,0:T(8,128)(2,1)}, u32[]{:S(2)}) copy-start(bf16[256,2048]{1,0:T(8,128)(2,1)} %param.12) | copy-start | bytes 3145732
  7.2 107.2 %all-gather.6.cloned.1.call-start = ((), (), s32[]{:S(2)}) async-start(), calls=%async_computation | async-start | bytes 13369344 | tf_op jit(solution)/shard_map/all_gather | solution.py:50
  9.4 187.7 %all-gather.8.cloned.1.call-start = ((), (), s32[]{:S(2)}) async-start(), calls=%async_computation.1 | async-start | bytes 8912896 | tf_op jit(solution)/shard_map/all_gather | solution.py:14
  122.5 1.6 copy-start.11
  122.7 13.8 %copy-start.2 = (bf16[32,8,8,128]{3,2,1,0:T(8,128)(2,1)}, bf16[32,8,8,128]{3,2,1,0:T(8,128)(2,1)S(1)}, u32[]{:S(2)}) copy-start(bf16[32,8,8,128]{3,2,1,0:T(8,128)(2,1)S(1)} %copy.131) | copy-start | bytes 1572868
  123.9 170.7 %all-gather.10.cloned.1.call-start = ((), (), s32[]{:S(2)}) async-start(), calls=%async_computation.2 | async-start | bytes 8912896 | tf_op jit(solution)/shard_map/all_gather | solution.py:14
  128.4 0.8 copy-start.8
  131.4 5.2 %copy-start.4 = (bf16[2,128,8,128,1]{1,3,0,4,2:T(8,128)(2,1)}, bf16[2,128,8,128,1]{1,3,0,4,2:T(8,128)(2,1)S(1)}, u32[]{:S(2)}) copy-start(bf16[2,128,8,128,1]{1,3,0,4,2:T(8,128)(2,1)S(1)} %copy.101) | copy-start | bytes 1572868
  136.6 1.7 copy-start.6
  138.3 1.0 copy-start
  197.1 20.1 %copy-start.7 = (bf16[2,128,8,128]{1,3,0,2:T(8,128)(2,1)S(1)}, bf16[2,128,8,128]{1,3,0,2:T(8,128)(2,1)}, u32[]{:S(2)}) copy-start(bf16[2,128,8,128]{1,3,0,2:T(8,128)(2,1)} %copy.79) | copy-start | bytes 1572868
  225.2 8.2 %copy-start.5 = (bf16[2,128,8,128,1]{1,3,0,4,2:T(8,128)(2,1)S(1)}, bf16[2,128,8,128,1]{1,3,0,4,2:T(8,128)(2,1)}, u32[]{:S(2)}) copy-start(bf16[2,128,8,128,1]{1,3,0,4,2:T(8,128)(2,1)} %copy-done.4) | copy-start | bytes 1572868
  231.4 3.5 %copy-start.1 = (bf16[8,2,2,128,128]{3,4,1,2,0:T(8,128)(2,1)S(1)}, bf16[8,2,2,128,128]{3,4,1,2,0:T(8,128)(2,1)}, u32[]{:S(2)}) copy-start(bf16[8,2,2,128,128]{3,4,1,2,0:T(8,128)(2,1)} %copy-done) | copy-start | bytes 3145732
  294.5 20.2 %copy-start.3 = (bf16[32,8,8,128]{3,2,1,0:T(8,128)(2,1)S(1)}, bf16[32,8,8,128]{3,2,1,0:T(8,128)(2,1)}, u32[]{:S(2)}) copy-start(bf16[32,8,8,128]{3,2,1,0:T(8,128)(2,1)} %copy-done.2) | copy-start | bytes 1572868
  317.5 1.0 copy-start.9
  317.8 1.1 copy-start.10
Sparse Core Ops, SparseCore 0:
  10.9 103.4 all-gather.5
  124.0 73.0 all-gather.7
  221.4 73.1 all-gather.9
where the time goes:
time: 337 us; the launch traced here: 334 us
  waiting for transfers between devices  221 us (66%)
  other arithmetic  44.2 us (13%)
  matrix products  31.5 us (9%)
  local copies, waits for them, and re-layouts  22.9 us (7%)
  between operations  14.1 us (4%)
    all_gather x2, waiting for transfers between devices, carried_in(): everything = lax.all_gather(shard, axis)  116 us
    all_gather x1, waiting for transfers between devices, on_device(): full_weights = lax.all_gather(w_cat, 'seq', axis=0, tiled=True)  105 us
    select_n x32, other arithmetic, turn(): return jnp.where(reached, new, before)  39.4 us
    unnamed x37, local copies, waits for them, and re-layouts  9.01 us
    dot_general x1, matrix products, on_device(): lax.dot_general(d_proj, full_weights, (((1,), (1,)), ((), ())), preferred...  8.99 us
    dot_general x1, matrix products, on_device(): projected = jnp.dot(x_in, full_weights, preferred_element_type=f32)  7.98 us
  transfers between devices with their start and end apart: 3, of which 3 were waited for; matrix products, arithmetic and copies ran while one was open for 9% of the time, Pallas kernels for 0%

commit v1 on v0

--- a/solution.py
+++ b/solution.py
@@ -2,6 +2,7 @@
 import jax.numpy as jnp
 from jax import lax
 from jax.sharding import PartitionSpec as P
+from jax.lax import axis_index, axis_size, ppermute
 
 NH = 8
 DH = 128
@@ -47,7 +48,19 @@
     f32 = jnp.float32
     x_in = (clean.astype(f32) + delta.astype(f32)).astype(jnp.bfloat16)
     w_cat = jnp.concatenate([w_query, w_key, w_value], axis=1)
-    full_weights = lax.all_gather(w_cat, "seq", axis=0, tiled=True)
+    n_shards = axis_size("seq")
+    history = [(j, (j + 1) % n_shards) for j in range(n_shards)]
+    chunks = [(j, (j - 1) % n_shards) for j in range(n_shards)]
+    z, block_next = ([w_cat], [w_cat])
+    for _ in range(n_shards // 2):
+        z.append(ppermute(z[-1], axis_name="seq", perm=history))
+    for _ in range((n_shards - 1) // 2):
+        block_next.append(ppermute(block_next[-1], axis_name="seq", perm=chunks))
+    full_weights = jnp.roll(
+        jnp.concatenate([*z[::-1], *block_next[1:]], 0),
+        (axis_index("seq") - n_shards // 2) * w_cat.shape[0],
+        0,
+    )
     projected = jnp.dot(x_in, full_weights, preferred_element_type=f32)
     projected = projected.astype(jnp.bfloat16)
     query = projected[:, :features].reshape(blocks_here, BLK, NH, DH)

time: 337 us -> 440 us (1.31)
  starting transfers between devices: 0.3 us -> 81.8 us
  local copies, waits for them, and re-layouts: 22.9 us -> 74.2 us
  waiting for transfers between devices: 221 us -> 188 us
  matrix products: 31.5 us -> 37 us
    all_gather x1 -> x0, waiting for transfers between devices: 105 us -> none  [on_device(): full_weights = lax.all_gather(w_cat, 'seq', axis=0, tiled=True)]
    ppermute x0 -> x15, starting transfers between devices: none -> 81.5 us  [the longest x8 75 us: on_device(): z.append(ppermute(z[-1], axis_name='seq', perm=history))]
    unnamed x37 -> x98, local copies, waits for them, and re-layouts: 9.01 us -> 59.9 us
    ppermute x0 -> x15, waiting for transfers between devices: none -> 50.6 us  [the longest x8 50.5 us: on_device(): z.append(ppermute(z[-1], axis_name='seq', perm=history))]
    all_gather x2, waiting for transfers between devices: 116 us -> 137 us  [carried_in(): everything = lax.all_gather(shard, axis)]
  transfers between devices with their start and end apart: 3 -> 17, of which waited for: 3 -> 10; matrix products, arithmetic and copies ran while one was open for 9% -> 13% of each run, Pallas kernels for 0% -> 0%
where the time goes in v1:
time: 440 us; the launch traced here: 437 us
  waiting for transfers between devices  188 us (43%)
  starting transfers between devices  81.8 us (19%)
  local copies, waits for them, and re-layouts  74.2 us (17%)
  other arithmetic  40.9 us (9%)
  matrix products  37 us (8%)
  between operations  14.5 us (3%)
    all_gather x2, waiting for transfers between devices, carried_in(): everything = lax.all_gather(shard, axis)  137 us
    ppermute x8, starting transfers between devices, on_device(): z.append(ppermute(z[-1], axis_name='seq', perm=history))  75 us
    unnamed x98, local copies, waits for them, and re-layouts  59.9 us
    ppermute x8, waiting for transfers between devices, on_device(): z.append(ppermute(z[-1], axis_name='seq', perm=history))  50.5 us
    select_n x32, other arithmetic, turn(): return jnp.where(reached, new, before)  39.3 us
    dot_general x1, matrix products, on_device(): lax.dot_general(d_proj, full_weights, (((1,), (1,)), ((), ())), preferred...  9.18 us
  transfers between devices with their start and end apart: 17, of which 10 were waited for; matrix products, arithmetic and copies ran while one was open for 13% of the time, Pallas kernels for 0%

profile of v1, /device:TPU:0, one launch (start us, length us, event | category | flops | bytes accessed | tf_op | source)
XLA Modules:
  0.0 437.0 jit_solution(2525454364516354044)
XLA Ops:
  10.7 14.7 %collective-permute-done = bf16[128,3072]{1,0:T(8,128)(2,1)S(1)} collective-permute-done((bf16[128,3072]{1,0:T(8,128)(2,1)S(1)}, bf16[128,3072]{1,0:T(8,128)(2,1)S(1)}, u32[]{:S(2)}, u32[]{:S(2)}) %collective-permute-start) | collective-permute-done | bytes 786464 | tf_op jit(solution)/shard_map/ppermute | solution.py:56
  25.3 4.4 %collective-permute-start.8 = (bf16[128,3072]{1,0:T(8,128)(2,1)S(1)}, bf16[128,3072]{1,0:T(8,128)(2,1)S(1)}, u32[]{:S(2)}, u32[]{:S(2)}) collective-permute-start(bf16[128,3072]{1,0:T(8,128)(2,1)S(1)} %constant_dynamic-update-slice_fusion), channel_id=1, source_target_pairs={{0,15},{1,0},{2,1},{3,2},{4,3},{5,4},{6,5},{7,6},{8,7},{9,8},{10,9... | collective-permute-start | bytes 2359304 | tf_op jit(solution)/shard_map/ppermute | solution.py:58
  29.8 9.8 %collective-permute-done.1 = bf16[128,3072]{1,0:T(8,128)(2,1)S(1)} collective-permute-done((bf16[128,3072]{1,0:T(8,128)(2,1)S(1)}, bf16[128,3072]{1,0:T(8,128)(2,1)S(1)}, u32[]{:S(2)}, u32[]{:S(2)}) %collective-permute-start.1) | collective-permute-done | bytes 786464 | tf_op jit(solution)/shard_map/ppermute | solution.py:56
  39.6 2.5 collective-permute-start.2
  42.1 1.9 collective-permute-start.9
  44.0 9.8 %collective-permute-done.2 = bf16[128,3072]{1,0:T(8,128)(2,1)S(1)} collective-permute-done((bf16[128,3072]{1,0:T(8,128)(2,1)S(1)}, bf16[128,3072]{1,0:T(8,128)(2,1)S(1)}, u32[]{:S(2)}, u32[]{:S(2)}) %collective-permute-start.2) | collective-permute-done | bytes 786464 | tf_op jit(solution)/shard_map/ppermute | solution.py:56
  53.8 7.4 %collective-permute-start.3 = (bf16[128,3072]{1,0:T(8,128)(2,1)S(1)}, bf16[128,3072]{1,0:T(8,128)(2,1)S(1)}, u32[]{:S(2)}, u32[]{:S(2)}) collective-permute-start(bf16[128,3072]{1,0:T(8,128)(2,1)S(1)} %collective-permute-done.2), channel_id=1, source_target_pairs={{0,1},{1,2},{2,3},{3,4},{4,5},{5,6},{6,7},{7,8},{8,9},{9,10},{10,1... | collective-permute-start | bytes 2359304 | tf_op jit(solution)/shard_map/ppermute | solution.py:56
  61.2 6.8 %collective-permute-done.3 = bf16[128,3072]{1,0:T(8,128)(2,1)S(1)} collective-permute-done((bf16[128,3072]{1,0:T(8,128)(2,1)S(1)}, bf16[128,3072]{1,0:T(8,128)(2,1)S(1)}, u32[]{:S(2)}, u32[]{:S(2)}) %collective-permute-start.3) | collective-permute-done | bytes 786464 | tf_op jit(solution)/shard_map/ppermute | solution.py:56
  68.0 13.0 %collective-permute-start.4 = (bf16[128,3072]{1,0:T(8,128)(2,1)S(1)}, bf16[128,3072]{1,0:T(8,128)(2,1)S(1)}, u32[]{:S(2)}, u32[]{:S(2)}) collective-permute-start(bf16[128,3072]{1,0:T(8,128)(2,1)S(1)} %collective-permute-done.3), channel_id=1, source_target_pairs={{0,1},{1,2},{2,3},{3,4},{4,5},{5,6},{6,7},{7,8},{8,9},{9,10},{10,1... | collective-permute-start | bytes 2359304 | tf_op jit(solution)/shard_map/ppermute | solution.py:56
  81.9 1.4 collective-permute-done.4
  83.3 17.6 %collective-permute-start.5 = (bf16[128,3072]{1,0:T(8,128)(2,1)S(1)}, bf16[128,3072]{1,0:T(8,128)(2,1)S(1)}, u32[]{:S(2)}, u32[]{:S(2)}) collective-permute-start(bf16[128,3072]{1,0:T(8,128)(2,1)S(1)} %collective-permute-done.4), channel_id=1, source_target_pairs={{0,1},{1,2},{2,3},{3,4},{4,5},{5,6},{6,7},{7,8},{8,9},{9,10},{10,1... | collective-permute-start | bytes 2359304 | tf_op jit(solution)/shard_map/ppermute | solution.py:56
  101.7 1.4 collective-permute-done.5
  103.2 17.5 %collective-permute-start.6 = (bf16[128,3072]{1,0:T(8,128)(2,1)S(1)}, bf16[128,3072]{1,0:T(8,128)(2,1)}, u32[]{:S(2)}, u32[]{:S(2)}) collective-permute-start(bf16[128,3072]{1,0:T(8,128)(2,1)S(1)} %collective-permute-done.5), channel_id=1, source_target_pairs={{0,1},{1,2},{2,3},{3,4},{4,5},{5,6},{6,7},{7,8},{8,9},{9,10},{10,1... | collective-permute-start | bytes 2359304 | tf_op jit(solution)/shard_map/ppermute | solution.py:56
  120.7 3.3 collective-permute-done.6
  124.0 16.6 %collective-permute-start.7 = (bf16[128,3072]{1,0:T(8,128)(2,1)}, bf16[128,3072]{1,0:T(8,128)(2,1)}, u32[]{:S(2)}, u32[]{:S(2)}) collective-permute-start(bf16[128,3072]{1,0:T(8,128)(2,1)} %collective-permute-done.6), channel_id=1, source_target_pairs={{0,1},{1,2},{2,3},{3,4},{4,5},{5,6},{6,7},{7,8},{8,9},{9,10},{10,1... | collective-permute-start | bytes 2359304 | tf_op jit(solution)/shard_map/ppermute | solution.py:56
  140.7 3.4 collective-permute-done.7
  144.1 2.1 constant_dynamic-update-slice_fusion.34
  146.2 2.1 constant_dynamic-update-slice_fusion.33
  148.3 2.1 constant_dynamic-update-slice_fusion.32
  150.3 2.1 constant_dynamic-update-slice_fusion.31
  152.4 2.1 constant_dynamic-update-slice_fusion.30
  154.5 2.1 constant_dynamic-update-slice_fusion.29
  158.5 1.7 constant_dynamic-update-slice_fusion.26
  160.2 1.7 constant_dynamic-update-slice_fusion.37
  161.8 1.7 constant_dynamic-update-slice_fusion.36
  165.5 2.1 constant_dynamic-update-slice_fusion.23
  167.6 2.1 constant_dynamic-update-slice_fusion.22
  169.7 2.1 constant_dynamic-update-slice_fusion.21
  171.8 2.1 constant_dynamic-update-slice_fusion.20
  174.9 2.1 constant_dynamic-update-slice_fusion.18
  176.9 2.1 constant_dynamic-update-slice_fusion.17
  190.8 2.1 constant_dynamic-update-slice_fusion.5
  192.9 2.1 constant_dynamic-update-slice_fusion.4
  195.9 8.1 %fusion.4 = bf16[256,3072]{1,0:T(8,128)(2,1)S(1)} fusion(bf16[4096,3072]{1,0:T(8,128)(2,1)} %constant_dynamic-update-slice_fusion.3, s32[]{:T(128)S(6)} %select_n.65, bf16[256,2048]{1,0:T(8,128)(2,1)S(1)} %copy-done.24, bf16[256,2048]{1,0:T(8,128)(2,1)S(1)} %copy-done.25), kind=kOutput, calls=%fused_computation.6 | convolution fusion | flops 3224109056 | bytes 16252932 | tf_op jit(solution)/shard_map/dot_general | solution.py:64
  207.3 1.6 copy.70
  210.7 1.4 copy.101
  213.0 2.1 copy.96
  215.1 2.1 copy.79
  217.3 1.7 fusion.11
  219.0 1.3 convolution_bitcast_fusion
  220.3 77.7 %all-gather.5.cloned.1.call-done = f32[128,128,128]{2,1,0:T(8,128)} async-done(((f32[8,128,128]{2,1,0:T(8,128)}), f32[128,128,128]{2,1,0:T(8,128)}) %all-gather.5.cloned.1.call-update) | async-done | bytes 8388624 | tf_op jit(solution)/shard_map/all_gather | solution.py:15
  298.0 20.0 %while.30 = (s32[]{:T(128)}, f32[8,128,128]{2,1,0:T(8,128)S(1)}, s32[]{:T(128)}, f32[16,8,128,128]{3,2,1,0:T(8,128)}, s32[]{:T(128)}, /*index=5*/s32[]{:T(128)}) while((s32[]{:T(128)}, f32[8,128,128]{2,1,0:T(8,128)S(1)}, s32[]{:T(128)}, f32[16,8,128,128]{3,2,1,0:T(8,128)}, s32[]{:T(128)}, /*index=5*/s32[]{:T(128)}) %tuple.87), condition=%wide.region_1.2_spmd.clone, body=%wide.region_0.1_spmd.clone.sunk | while | flops 393220 | bytes 1572957 | solution.py:24
  299.3 1.2 add_select_fusion.4
  300.5 1.2 add_select_fusion.4
  301.8 1.2 add_select_fusion.4
  303.0 1.2 add_select_fusion.4
  304.3 1.2 add_select_fusion.4
  305.5 1.2 add_select_fusion.4
  306.8 1.2 add_select_fusion.4
  308.0 1.2 add_select_fusion.4
  318.0 1.7 multiply_reduce_fusion.1
  321.2 2.2 convolution_bitcast_fusion.4
  323.4 1.5 fusion.10
  325.9 1.4 convolution_bitcast_fusion.3
  328.3 1.4 copy.76
  330.6 1.4 copy.68
  332.9 2.9 convolution_bitcast_fusion.2
  335.7 1.4 convolution_bitcast_fusion.1
  337.2 59.6 %all-gather.7.cloned.1.call-done = f32[128,128,128]{2,1,0:T(8,128)} async-done(((f32[8,128,128]{2,1,0:T(8,128)}), f32[128,128,128]{2,1,0:T(8,128)}) %all-gather.7.cloned.1.call-update) | async-done | bytes 8388624 | tf_op jit(solution)/shard_map/all_gather | solution.py:15
  396.7 20.1 %while.31 = (s32[]{:T(128)}, f32[8,128,128]{2,1,0:T(8,128)S(1)}, s32[]{:T(128)}, f32[16,8,128,128]{3,2,1,0:T(8,128)}, s32[]{:T(128)}, /*index=5*/s32[]{:T(128)}, s32[]{:T(128)}, s32[]{:T(128)}) while((s32[]{:T(128)}, f32[8,128,128]{2,1,0:T(8,128)S(1)}, s32[]{:T(128)}, f32[16,8,128,128]{3,2,1,0:T(8,128)}, s32[]{:T(128)}, ...), condition=%wide.region_5.6_spmd.clone, body=%wide.region_4.5_spmd.clone.sunk | while | flops 393224 | bytes 1573019 | solution.py:24
  401.7 1.2 add_select_fusion.5
  416.8 1.5 fusion.22
  418.8 1.7 fusion.21
  420.9 9.2 %fusion.7 = bf16[256,2048]{1,0:T(8,128)(2,1)} fusion(bf16[4096,3072]{1,0:T(8,128)(2,1)} %constant_dynamic-update-slice_fusion.3, s32[]{:T(128)S(6)} %select_n.65, bf16[256,1024]{1,0:T(8,128)(2,1)S(1)} %bitcast.165, bf16[256,1024]{1,0:T(8,128)(2,1)S(1)} %bitcast.164, bf16[256,1024]{1,0:T(8,128)(2,1)} %bitcast.163), kind=kOutput, calls=%fused_computation.7 | convolution fusion | flops 3226468352 | bytes 15204356 | tf_op jit(solution)/shard_map/dot_general | solution.py:104
  (143 shorter events, 63.2 us)
Async XLA Ops:
  7.2 177.6 %copy-start.19 = (bf16[128,1024]{1,0:T(8,128)(2,1)S(1)}, bf16[128,1024]{1,0:T(8,128)(2,1)}, u32[]{:S(2)}) copy-start(bf16[128,1024]{1,0:T(8,128)(2,1)} %param.14) | copy-start | bytes 786436
  7.2 290.8 %all-gather.5.cloned.1.call-start = ((), (), s32[]{:S(2)}) async-start(), calls=%async_computation | async-start | bytes 8912896 | tf_op jit(solution)/shard_map/all_gather | solution.py:15
  10.2 15.2 %collective-permute-start = (bf16[128,3072]{1,0:T(8,128)(2,1)S(1)}, bf16[128,3072]{1,0:T(8,128)(2,1)S(1)}, u32[]{:S(2)}, u32[]{:S(2)}) collective-permute-start(bf16[128,3072]{1,0:T(8,128)(2,1)S(1)} %constant_dynamic-update-slice_fusion), channel_id=1, source_target_pairs={{0,1},{1,2},{2,3},{3,4},{4,5},{5,6},{6,7},{7,8},{8,9},{9,10},{10,1... | collective-permute-start | bytes 2359304 | tf_op jit(solution)/shard_map/ppermute | solution.py:56
  25.3 14.2 %collective-permute-start.1 = (bf16[128,3072]{1,0:T(8,128)(2,1)S(1)}, bf16[128,3072]{1,0:T(8,128)(2,1)S(1)}, u32[]{:S(2)}, u32[]{:S(2)}) collective-permute-start(bf16[128,3072]{1,0:T(8,128)(2,1)S(1)} %collective-permute-done), channel_id=1, source_target_pairs={{0,1},{1,2},{2,3},{3,4},{4,5},{5,6},{6,7},{7,8},{8,9},{9,10},{10,1... | collective-permute-start | bytes 2359304 | tf_op jit(solution)/shard_map/ppermute | solution.py:56
  25.3 16.7 %collective-permute-start.8 = (bf16[128,3072]{1,0:T(8,128)(2,1)S(1)}, bf16[128,3072]{1,0:T(8,128)(2,1)S(1)}, u32[]{:S(2)}, u32[]{:S(2)}) collective-permute-start(bf16[128,3072]{1,0:T(8,128)(2,1)S(1)} %constant_dynamic-update-slice_fusion), channel_id=1, source_target_pairs={{0,15},{1,0},{2,1},{3,2},{4,3},{5,4},{6,5},{7,6},{8,7},{9,8},{10,9... | collective-permute-start | bytes 2359304 | tf_op jit(solution)/shard_map/ppermute | solution.py:58
  39.6 14.2 %collective-permute-start.2 = (bf16[128,3072]{1,0:T(8,128)(2,1)S(1)}, bf16[128,3072]{1,0:T(8,128)(2,1)S(1)}, u32[]{:S(2)}, u32[]{:S(2)}) collective-permute-start(bf16[128,3072]{1,0:T(8,128)(2,1)S(1)} %collective-permute-done.1), channel_id=1, source_target_pairs={{0,1},{1,2},{2,3},{3,4},{4,5},{5,6},{6,7},{7,8},{8,9},{9,10},{10,1... | collective-permute-start | bytes 2359304 | tf_op jit(solution)/shard_map/ppermute | solution.py:56
  42.1 19.1 %collective-permute-start.9 = (bf16[128,3072]{1,0:T(8,128)(2,1)S(1)}, bf16[128,3072]{1,0:T(8,128)(2,1)S(1)}, u32[]{:S(2)}, u32[]{:S(2)}) collective-permute-start(bf16[128,3072]{1,0:T(8,128)(2,1)S(1)} %collective-permute-done.8), channel_id=1, source_target_pairs={{0,15},{1,0},{2,1},{3,2},{4,3},{5,4},{6,5},{7,6},{8,7},{9,8},{10,9... | collective-permute-start | bytes 2359304 | tf_op jit(solution)/shard_map/ppermute | solution.py:58
  53.8 27.2 %copy-start.7 = (bf16[128,3072]{1,0:T(8,128)(2,1)}, bf16[128,3072]{1,0:T(8,128)(2,1)S(1)}, u32[]{:S(2)}) copy-start(bf16[128,3072]{1,0:T(8,128)(2,1)S(1)} %collective-permute-done.2) | copy-start | bytes 2359300
  53.8 14.2 %collective-permute-start.3 = (bf16[128,3072]{1,0:T(8,128)(2,1)S(1)}, bf16[128,3072]{1,0:T(8,128)(2,1)S(1)}, u32[]{:S(2)}, u32[]{:S(2)}) collective-permute-start(bf16[128,3072]{1,0:T(8,128)(2,1)S(1)} %collective-permute-done.2), channel_id=1, source_target_pairs={{0,1},{1,2},{2,3},{3,4},{4,5},{5,6},{6,7},{7,8},{8,9},{9,10},{10,1... | collective-permute-start | bytes 2359304 | tf_op jit(solution)/shard_map/ppermute | solution.py:56
  61.2 19.8 %collective-permute-start.10 = (bf16[128,3072]{1,0:T(8,128)(2,1)S(1)}, bf16[128,3072]{1,0:T(8,128)(2,1)S(1)}, u32[]{:S(2)}, u32[]{:S(2)}) collective-permute-start(bf16[128,3072]{1,0:T(8,128)(2,1)S(1)} %collective-permute-done.9), channel_id=1, source_target_pairs={{0,15},{1,0},{2,1},{3,2},{4,3},{5,4},{6,5},{7,6},{8,7},{9,8},{10,9... | collective-permute-start | bytes 2359304 | tf_op jit(solution)/shard_map/ppermute | solution.py:58
  68.0 52.7 %copy-start.13 = (bf16[128,3072]{1,0:T(8,128)(2,1)}, bf16[128,3072]{1,0:T(8,128)(2,1)S(1)}, u32[]{:S(2)}) copy-start(bf16[128,3072]{1,0:T(8,128)(2,1)S(1)} %collective-permute-done.3) | copy-start | bytes 2359300
  68.0 15.3 %collective-permute-start.4 = (bf16[128,3072]{1,0:T(8,128)(2,1)S(1)}, bf16[128,3072]{1,0:T(8,128)(2,1)S(1)}, u32[]{:S(2)}, u32[]{:S(2)}) collective-permute-start(bf16[128,3072]{1,0:T(8,128)(2,1)S(1)} %collective-permute-done.3), channel_id=1, source_target_pairs={{0,1},{1,2},{2,3},{3,4},{4,5},{5,6},{6,7},{7,8},{8,9},{9,10},{10,1... | collective-permute-start | bytes 2359304 | tf_op jit(solution)/shard_map/ppermute | solution.py:56
  81.0 0.9 copy-start.9
  81.0 19.8 %collective-permute-start.11 = (bf16[128,3072]{1,0:T(8,128)(2,1)S(1)}, bf16[128,3072]{1,0:T(8,128)(2,1)S(1)}, u32[]{:S(2)}, u32[]{:S(2)}) collective-permute-start(bf16[128,3072]{1,0:T(8,128)(2,1)S(1)} %collective-permute-done.10), channel_id=1, source_target_pairs={{0,15},{1,0},{2,1},{3,2},{4,3},{5,4},{6,5},{7,6},{8,7},{9,8},{10,9... | collective-permute-start | bytes 2359304 | tf_op jit(solution)/shard_map/ppermute | solution.py:58
  83.3 37.4 %copy-start.15 = (bf16[128,3072]{1,0:T(8,128)(2,1)}, bf16[128,3072]{1,0:T(8,128)(2,1)S(1)}, u32[]{:S(2)}) copy-start(bf16[128,3072]{1,0:T(8,128)(2,1)S(1)} %collective-permute-done.4) | copy-start | bytes 2359300
  83.3 19.9 %collective-permute-start.5 = (bf16[128,3072]{1,0:T(8,128)(2,1)S(1)}, bf16[128,3072]{1,0:T(8,128)(2,1)S(1)}, u32[]{:S(2)}, u32[]{:S(2)}) collective-permute-start(bf16[128,3072]{1,0:T(8,128)(2,1)S(1)} %collective-permute-done.4), channel_id=1, source_target_pairs={{0,1},{1,2},{2,3},{3,4},{4,5},{5,6},{6,7},{7,8},{8,9},{9,10},{10,1... | collective-permute-start | bytes 2359304 | tf_op jit(solution)/shard_map/ppermute | solution.py:56
  100.9 0.9 copy-start.11
  101.7 19.0 %collective-permute-start.12 = (bf16[128,3072]{1,0:T(8,128)(2,1)S(1)}, bf16[128,3072]{1,0:T(8,128)(2,1)}, u32[]{:S(2)}, u32[]{:S(2)}) collective-permute-start(bf16[128,3072]{1,0:T(8,128)(2,1)S(1)} %collective-permute-done.11), channel_id=1, source_target_pairs={{0,15},{1,0},{2,1},{3,2},{4,3},{5,4},{6,5},{7,6},{8,7},{9,8},{10,9... | collective-permute-start | bytes 2359304 | tf_op jit(solution)/shard_map/ppermute | solution.py:58
  103.2 20.8 %copy-start.17 = (bf16[128,3072]{1,0:T(8,128)(2,1)}, bf16[128,3072]{1,0:T(8,128)(2,1)S(1)}, u32[]{:S(2)}) copy-start(bf16[128,3072]{1,0:T(8,128)(2,1)S(1)} %collective-permute-done.5) | copy-start | bytes 2359300
  103.2 20.8 %collective-permute-start.6 = (bf16[128,3072]{1,0:T(8,128)(2,1)S(1)}, bf16[128,3072]{1,0:T(8,128)(2,1)}, u32[]{:S(2)}, u32[]{:S(2)}) collective-permute-start(bf16[128,3072]{1,0:T(8,128)(2,1)S(1)} %collective-permute-done.5), channel_id=1, source_target_pairs={{0,1},{1,2},{2,3},{3,4},{4,5},{5,6},{6,7},{7,8},{8,9},{9,10},{10,1... | collective-permute-start | bytes 2359304 | tf_op jit(solution)/shard_map/ppermute | solution.py:56
  120.7 19.9 %collective-permute-start.13 = (bf16[128,3072]{1,0:T(8,128)(2,1)}, bf16[128,3072]{1,0:T(8,128)(2,1)}, u32[]{:S(2)}, u32[]{:S(2)}) collective-permute-start(bf16[128,3072]{1,0:T(8,128)(2,1)} %collective-permute-done.12), channel_id=1, source_target_pairs={{0,15},{1,0},{2,1},{3,2},{4,3},{5,4},{6,5},{7,6},{8,7},{9,8},{10,9... | collective-permute-start | bytes 2359304 | tf_op jit(solution)/shard_map/ppermute | solution.py:58
  124.0 20.1 %collective-permute-start.7 = (bf16[128,3072]{1,0:T(8,128)(2,1)}, bf16[128,3072]{1,0:T(8,128)(2,1)}, u32[]{:S(2)}, u32[]{:S(2)}) collective-permute-start(bf16[128,3072]{1,0:T(8,128)(2,1)} %collective-permute-done.6), channel_id=1, source_target_pairs={{0,1},{1,2},{2,3},{3,4},{4,5},{5,6},{6,7},{7,8},{8,9},{9,10},{10,1... | collective-permute-start | bytes 2359304 | tf_op jit(solution)/shard_map/ppermute | solution.py:56
  140.5 38.4 %copy-start.18 = (bf16[128,3072]{1,0:T(8,128)(2,1)S(1)}, bf16[128,3072]{1,0:T(8,128)(2,1)}, u32[]{:S(2)}) copy-start(bf16[128,3072]{1,0:T(8,128)(2,1)} %copy-done.17) | copy-start | bytes 2359300
  140.5 39.4 %copy-start.16 = (bf16[128,3072]{1,0:T(8,128)(2,1)S(1)}, bf16[128,3072]{1,0:T(8,128)(2,1)}, u32[]{:S(2)}) copy-start(bf16[128,3072]{1,0:T(8,128)(2,1)} %copy-done.15) | copy-start | bytes 2359300
  140.5 40.3 %copy-start.14 = (bf16[128,3072]{1,0:T(8,128)(2,1)S(1)}, bf16[128,3072]{1,0:T(8,128)(2,1)}, u32[]{:S(2)}) copy-start(bf16[128,3072]{1,0:T(8,128)(2,1)} %copy-done.13) | copy-start | bytes 2359300
  140.5 41.3 %copy-start.8 = (bf16[128,3072]{1,0:T(8,128)(2,1)S(1)}, bf16[128,3072]{1,0:T(8,128)(2,1)}, u32[]{:S(2)}) copy-start(bf16[128,3072]{1,0:T(8,128)(2,1)} %copy-done.7) | copy-start | bytes 2359300
  140.5 45.0 %copy-start.20 = (bf16[128,1024]{1,0:T(8,128)(2,1)S(1)}, bf16[128,1024]{1,0:T(8,128)(2,1)}, u32[]{:S(2)}) copy-start(bf16[128,1024]{1,0:T(8,128)(2,1)} %param.15) | copy-start | bytes 786436
  140.6 45.7 %copy-start.21 = (bf16[128,1024]{1,0:T(8,128)(2,1)S(1)}, bf16[128,1024]{1,0:T(8,128)(2,1)}, u32[]{:S(2)}) copy-start(bf16[128,1024]{1,0:T(8,128)(2,1)} %param.16) | copy-start | bytes 786436
  140.6 48.3 %copy-start.10 = (bf16[128,3072]{1,0:T(8,128)(2,1)S(1)}, bf16[128,3072]{1,0:T(8,128)(2,1)}, u32[]{:S(2)}) copy-start(bf16[128,3072]{1,0:T(8,128)(2,1)} %copy-done.9) | copy-start | bytes 2359300
  140.6 49.2 %copy-start.12 = (bf16[128,3072]{1,0:T(8,128)(2,1)S(1)}, bf16[128,3072]{1,0:T(8,128)(2,1)}, u32[]{:S(2)}) copy-start(bf16[128,3072]{1,0:T(8,128)(2,1)} %copy-done.11) | copy-start | bytes 2359300
  140.6 55.3 %copy-start.24 = (bf16[256,2048]{1,0:T(8,128)(2,1)S(1)}, bf16[256,2048]{1,0:T(8,128)(2,1)}, u32[]{:S(2)}) copy-start(bf16[256,2048]{1,0:T(8,128)(2,1)} %param.12) | copy-start | bytes 3145732
  140.6 55.3 %copy-start.25 = (bf16[256,2048]{1,0:T(8,128)(2,1)S(1)}, bf16[256,2048]{1,0:T(8,128)(2,1)}, u32[]{:S(2)}) copy-start(bf16[256,2048]{1,0:T(8,128)(2,1)} %param.11) | copy-start | bytes 3145732
  140.6 33.3 %collective-permute-start.14 = (bf16[128,3072]{1,0:T(8,128)(2,1)}, bf16[128,3072]{1,0:T(8,128)(2,1)S(1)}, u32[]{:S(2)}, u32[]{:S(2)}) collective-permute-start(bf16[128,3072]{1,0:T(8,128)(2,1)} %collective-permute-done.13), channel_id=1, source_target_pairs={{0,15},{1,0},{2,1},{3,2},{4,3},{5,4},{6,5},{7,6},{8,7},{9,8},{10,9... | collective-permute-start | bytes 2359304 | tf_op jit(solution)/shard_map/ppermute | solution.py:58
  195.9 9.9 %copy-start.23 = (s32[1,2,2]{2,1,0:T(2,128)S(1)}, s32[1,2,2]{2,1,0:T(2,128)}, u32[]{:S(2)}) copy-start(s32[1,2,2]{2,1,0:T(2,128)} %param.17) | copy-start | bytes 52
  195.9 10.0 %copy-start.22 = (bf16[256,1024]{1,0:T(8,128)(2,1)S(1)}, bf16[256,1024]{1,0:T(8,128)(2,1)}, u32[]{:S(2)}) copy-start(bf16[256,1024]{1,0:T(8,128)(2,1)} %param.13) | copy-start | bytes 1572868
  204.3 12.9 %copy-start.2 = (bf16[32,8,8,128]{3,2,1,0:T(8,128)(2,1)}, bf16[32,8,8,128]{3,2,1,0:T(8,128)(2,1)S(1)}, u32[]{:S(2)}) copy-start(bf16[32,8,8,128]{3,2,1,0:T(8,128)(2,1)S(1)} %copy.131) | copy-start | bytes 1572868
  204.4 12.8 %copy-start.1 = (bf16[32,8,8,128]{3,2,1,0:T(8,128)(2,1)}, bf16[32,8,8,128]{3,2,1,0:T(8,128)(2,1)S(1)}, u32[]{:S(2)}) copy-start(bf16[32,8,8,128]{3,2,1,0:T(8,128)(2,1)S(1)} %copy.132) | copy-start | bytes 1572868
  205.6 191.1 %all-gather.7.cloned.1.call-start = ((), (), s32[]{:S(2)}) async-start(), calls=%async_computation.1 | async-start | bytes 8912896 | tf_op jit(solution)/shard_map/all_gather | solution.py:15
  209.1 0.8 copy-start.6
  212.1 108.0 %copy-start.4 = (bf16[2,128,8,128,1]{1,3,0,4,2:T(8,128)(2,1)}, bf16[2,128,8,128,1]{1,3,0,4,2:T(8,128)(2,1)S(1)}, u32[]{:S(2)}) copy-start(bf16[2,128,8,128,1]{1,3,0,4,2:T(8,128)(2,1)S(1)} %copy.101) | copy-start | bytes 1572868
  217.2 1.7 copy-start.5
  321.2 95.6 %copy-start.3 = (bf16[32,8,8,128]{3,2,1,0:T(8,128)(2,1)S(1)}, bf16[32,8,8,128]{3,2,1,0:T(8,128)(2,1)}, u32[]{:S(2)}) copy-start(bf16[32,8,8,128]{3,2,1,0:T(8,128)(2,1)} %copy-done.2) | copy-start | bytes 1572868
  324.9 1.0 copy-start
Sparse Core Ops, SparseCore 0:
  205.7 92.2 all-gather.4
  323.5 73.1 all-gather.6
